TPU v7x, 512 devices: a whole 4x4x16 slice. The times are simulated.
512 devices in a mesh: adapter: 64 (over y, z), mp: 8 (over x, core).
Axes of the slice: x: 4, y: 4, z: 16, core: 2. Of those that a mesh axis runs over, the one named last changes fastest.
Arguments:
- tokens: bfloat16 [24576, 8192], P('adapter', 'mp'), may hold values from -6 to 6
- cotangent: bfloat16 [24576, 1024], P('adapter', 'mp'), may hold values from -6 to 6
- value_weight: bfloat16 [8192, 1024], P('mp', 'adapter'), may hold values from -0.0625 to 0.0625
- down_store: bfloat16 [128, 8, 1024, 64], P(None, 'mp', 'adapter'), may hold values from -0.0625 to 0.0625
- down_first: float32 [128, 8, 1024, 64], P(None, 'mp', 'adapter'), may hold values from -4 to 4
- down_second: float32 [128, 8, 1024, 64], P(None, 'mp', 'adapter'), may hold values from 0.01 to 1
- up_store: bfloat16 [128, 64, 1024], P(None, 'adapter', 'mp'), may hold values from -0.75 to 0.75
- up_first: float32 [128, 64, 1024], P(None, 'adapter', 'mp'), may hold values from -4 to 4
- up_second: float32 [128, 64, 1024], P(None, 'adapter', 'mp'), may hold values from 0.01 to 1
- tile_adapter: int32 [192], replicated, may hold values from 0 to 127
- tile_length: int32 [192], replicated, may hold values from 1 to 128, as said below
- adapter_slot: int32 [128], replicated, may hold values from 0 to 127, each once
Outputs:
- projected: bfloat16 [24576, 1024], P('adapter', 'mp')
- token_gradient: bfloat16 [24576, 8192], P('adapter', 'mp')
- new_down: float32 [128, 8, 1024, 64], P(None, 'mp', 'adapter')
- new_down_first: float32 [128, 8, 1024, 64], P(None, 'mp', 'adapter')
- new_down_second: float32 [128, 8, 1024, 64], P(None, 'mp', 'adapter')
- new_up: float32 [128, 64, 1024], P(None, 'adapter', 'mp')
- new_up_first: float32 [128, 64, 1024], P(None, 'adapter', 'mp')
- new_up_second: float32 [128, 64, 1024], P(None, 'adapter', 'mp')
Inputs may be any that keep to these rules, and one draw needn't show every extreme that they name: `tile_length`: some tile is full in every draw. `adapter_slot`: each slot holds exactly one adapter.
All inputs are finite; a program needn't handle non-finite values.
Results may differ from a plain program's by a relative error of at most 0.0046.
Values may be sent and summed in bfloat16 or wider, within the bound.
No kernel may reach another device: no remote copies, remote signals or barrier semaphores. Data moves between devices by JAX's collectives and lax.ppermute only.
A program may use at most 64 MiB of HBM per device.

v0:
```python
import jax
import jax.numpy as jnp
from jax import lax
from jax.sharding import Mesh, PartitionSpec as P

TILE = 128
STEP = 100
adapter_scale = 2.0
learn_rate = 0.001
beta_one = 0.9
beta_two = 0.999
adam_eps = 1e-08


def adam_step(store, first, second, gradient):
    new_first = beta_one * first + (1.0 - beta_one) * gradient
    new_second = beta_two * second + (1.0 - beta_two) * gradient * gradient
    corr_one = 1.0 - beta_one**STEP
    corr_two = 1.0 - beta_two**STEP
    moved = store.astype(jnp.float32) - learn_rate * (new_first / corr_one) / (
        jnp.sqrt(new_second / corr_two) + adam_eps
    )
    return (moved, new_first, new_second)


ADAPTER = ("ay", "az")


def gather_along(piece, axis):
    count = lax.axis_size(axis)
    got = [piece]
    for shift in range(1, count):
        pairs = [(j, (j - shift) % count) for j in range(count)]
        got.append(lax.ppermute(piece, axis, pairs))
    ordered = jnp.roll(jnp.stack(got), lax.axis_index(axis), axis=0)
    return jnp.moveaxis(ordered, 0, 1).reshape(piece.shape[0], count * piece.shape[1])


def gather_weight(value_weight):
    return gather_along(gather_along(value_weight, "az"), "ay")


def split_adapter(mesh):
    devices = mesh.devices
    n_adapter = devices.shape[0]
    try:
        n_y = len({d.coords[1] for d in devices[:, 0]})
    except (AttributeError, IndexError, TypeError):
        n_y = 1
    if n_y < 1 or n_adapter % n_y:
        n_y = 1
    return Mesh(devices.reshape(n_y, n_adapter // n_y, devices.shape[1]), ("ay", "az", "mp"))


def shards(
    tokens,
    cotangent,
    value_weight,
    down_store,
    down_first,
    down_second,
    up_store,
    up_first,
    up_second,
    tile_adapter,
    tile_length,
    adapter_slot,
):
    tile_total = tile_adapter.shape[0]
    tok_count, feat_part = tokens.shape
    head_cols = cotangent.shape[1]
    tiles_here = tok_count // TILE
    adapter_count = adapter_slot.shape[0]
    my_index = lax.axis_index(ADAPTER)
    adapter_ids = jnp.arange(adapter_count, dtype=jnp.int32)
    tile_adapter_slot = jnp.sum(
        jnp.where(tile_adapter[:, None] == adapter_ids[None, :], adapter_slot[None, :], 0), axis=1
    )
    my_lengths = lax.dynamic_slice_in_dim(tile_length, my_index * tiles_here, tiles_here)
    active_rows = (jnp.arange(TILE)[None, :] < my_lengths[:, None]).reshape(tok_count, 1)
    masked_own = cotangent * active_rows.astype(jnp.bfloat16)
    masked_full = lax.all_gather(masked_own, "mp", axis=1, tiled=True)
    n_adapter = tile_total // tiles_here
    row_part = down_store.shape[2]
    rank = down_store.shape[3]
    sent_down = down_store[:, 0][tile_adapter_slot].reshape(tile_total, row_part * rank)
    sent_up = up_store[tile_adapter_slot].reshape(tile_total, head_cols)
    sent = jnp.concatenate([sent_down, sent_up], axis=1)
    arrived = lax.all_to_all(sent, ADAPTER, split_axis=0, concat_axis=0, tiled=True)
    arrived = arrived.reshape(n_adapter, tiles_here, row_part * rank + head_cols)
    down_panel = (
        arrived[:, :, : row_part * rank]
        .reshape(n_adapter, tiles_here, row_part, rank)
        .transpose(1, 0, 2, 3)
        .reshape(tiles_here, n_adapter * row_part, rank)
    )
    up_panel = arrived[:, :, row_part * rank :].transpose(1, 0, 2)
    w_full = gather_weight(value_weight)
    token_tiles = tokens.reshape(tiles_here, TILE, feat_part)
    frozen_part = jnp.dot(tokens, w_full, preferred_element_type=jnp.float32)
    frozen_local = lax.psum_scatter(frozen_part, "mp", scatter_dimension=1, tiled=True)
    down_part = jnp.einsum(
        "ntd,ndr->ntr", token_tiles, down_panel, preferred_element_type=jnp.float32
    )
    down_sum = lax.psum(down_part, "mp")
    down_portion = down_sum.astype(jnp.bfloat16)
    adapter_term = jnp.einsum(
        "ntr,nrv->ntv", down_portion, up_panel, preferred_element_type=jnp.float32
    ).reshape(tok_count, head_cols)
    projected = (
        (frozen_local + adapter_scale * adapter_term) * active_rows.astype(jnp.float32)
    ).astype(jnp.bfloat16)
    tile_mask = masked_own.reshape(tiles_here, TILE, head_cols)
    backward_piece = adapter_scale * jnp.einsum(
        "ntv,nrv->ntr", tile_mask, up_panel, preferred_element_type=jnp.float32
    )
    backward_portion = lax.psum(backward_piece, "mp").astype(jnp.bfloat16)
    frozen_backward = lax.dot_general(
        masked_full, w_full, (((1,), (1,)), ((), ())), preferred_element_type=jnp.float32
    )
    adapter_backward = jnp.einsum(
        "ntr,ndr->ntd", backward_portion, down_panel, preferred_element_type=jnp.float32
    ).reshape(tok_count, feat_part)
    token_gradient = (frozen_backward + adapter_backward).astype(jnp.bfloat16)
    home_down = jnp.einsum(
        "ntd,ntr->ndr", token_tiles, backward_portion, preferred_element_type=jnp.float32
    )
    local_up_weight = adapter_scale * jnp.einsum(
        "ntr,ntv->nrv", down_portion, tile_mask, preferred_element_type=jnp.float32
    )
    grads = jnp.concatenate(
        [home_down.reshape(tiles_here, n_adapter, row_part * rank), local_up_weight], axis=2
    )
    grads = lax.all_to_all(grads, ADAPTER, split_axis=1, concat_axis=0, tiled=True)
    arrived_down = grads[:, 0, : row_part * rank]
    arrived_up = grads[:, 0, row_part * rank :]
    selector = (adapter_ids[:, None] == tile_adapter_slot[None, :]).astype(jnp.float32)
    down_gradient = jnp.dot(
        selector, arrived_down.reshape(tile_total, -1), precision=lax.Precision.HIGHEST
    ).reshape(down_store.shape)
    up_gradient = jnp.dot(
        selector, arrived_up.reshape(tile_total, -1), precision=lax.Precision.HIGHEST
    ).reshape(up_store.shape)
    new_down, new_down_first, new_down_second = adam_step(
        down_store, down_first, down_second, down_gradient
    )
    new_up, new_up_first, new_up_second = adam_step(up_store, up_first, up_second, up_gradient)
    return (
        projected,
        token_gradient,
        new_down,
        new_down_first,
        new_down_second,
        new_up,
        new_up_first,
        new_up_second,
    )


def solution(mesh):
    mesh = split_adapter(mesh)
    placed = (
        P(ADAPTER, "mp"),
        P(ADAPTER, "mp"),
        P("mp", ADAPTER),
        P(None, "mp", ADAPTER, None),
        P(None, "mp", ADAPTER, None),
        P(None, "mp", ADAPTER, None),
        P(None, ADAPTER, "mp"),
        P(None, ADAPTER, "mp"),
        P(None, ADAPTER, "mp"),
        P(),
        P(),
        P(),
    )
    return jax.shard_map(
        shards,
        mesh=mesh,
        in_specs=placed,
        out_specs=(
            P(ADAPTER, "mp"),
            P(ADAPTER, "mp"),
            P(None, "mp", ADAPTER, None),
            P(None, "mp", ADAPTER, None),
            P(None, "mp", ADAPTER, None),
            P(None, ADAPTER, "mp"),
            P(None, ADAPTER, "mp"),
            P(None, ADAPTER, "mp"),
        ),
        check_vma=False,
    )
```

profile of v0, /device:TPU:6, one launch (start us, length us, event | category | flops | bytes accessed | tf_op | source)
XLA Modules:
  0.0 261.7 jit_solution(3475305058610863027)
XLA Ops:
  7.2 11.5 %collective-permute-start = (bf16[1024,16]{0,1:T(8,128)(2,1)}, bf16[1024,16]{0,1:T(8,128)(2,1)S(1)}, u32[]{:S(2)}, u32[]{:S(2)}) collective-permute-start(bf16[1024,16]{0,1:T(8,128)(2,1)} %param.14), channel_id=1, source_target_pairs={{0,120},{8,0},{16,8},{24,16},{32,24},{40,32},{48,40},{56,48},{64,5... | collective-permute-start | bytes 98312 | tf_op jit(solution)/shard_map/ppermute | solution.py:34
  18.7 3.4 %collective-permute-start.1 = (bf16[1024,16]{0,1:T(8,128)(2,1)}, bf16[1024,16]{0,1:T(8,128)(2,1)S(1)}, u32[]{:S(2)}, u32[]{:S(2)}) collective-permute-start(bf16[1024,16]{0,1:T(8,128)(2,1)} %param.14), channel_id=1, source_target_pairs={{0,112},{8,120},{16,0},{24,8},{32,16},{40,24},{48,32},{56,40},{64,... | collective-permute-start | bytes 98312 | tf_op jit(solution)/shard_map/ppermute | solution.py:34
  22.1 5.0 %collective-permute-start.2 = (bf16[1024,16]{0,1:T(8,128)(2,1)}, bf16[1024,16]{0,1:T(8,128)(2,1)S(1)}, u32[]{:S(2)}, u32[]{:S(2)}) collective-permute-start(bf16[1024,16]{0,1:T(8,128)(2,1)} %param.14), channel_id=1, source_target_pairs={{0,104},{8,112},{16,120},{24,0},{32,8},{40,16},{48,24},{56,32},{64... | collective-permute-start | bytes 98312 | tf_op jit(solution)/shard_map/ppermute | solution.py:34
  27.1 2.8 %collective-permute-start.3 = (bf16[1024,16]{0,1:T(8,128)(2,1)}, bf16[1024,16]{0,1:T(8,128)(2,1)S(1)}, u32[]{:S(2)}, u32[]{:S(2)}) collective-permute-start(bf16[1024,16]{0,1:T(8,128)(2,1)} %param.14), channel_id=1, source_target_pairs={{0,96},{8,104},{16,112},{24,120},{32,0},{40,8},{48,16},{56,24},{64... | collective-permute-start | bytes 98312 | tf_op jit(solution)/shard_map/ppermute | solution.py:34
  30.0 1.9 collective-permute-start.4
  38.1 15.8 %all-to-all-start = ((bf16[64,3,1152]{2,1,0:T(4,128)(2,1)}), bf16[64,3,1152]{2,1,0:T(4,128)(2,1)S(1)}, u32[]{:S(2)}, u32[]{:S(2)}) async-start(bf16[64,3,1152]{2,1,0:T(4,128)(2,1)} %pad_maximum_fusion.1), calls=%async_computation.1 | async-start | bytes 1179648 | tf_op jit(solution)/shard_map/all_to_all | solution.py:89
  54.0 10.4 %collective-permute-start.5 = (bf16[1024,16]{0,1:T(8,128)(2,1)S(1)}, bf16[1024,16]{0,1:T(8,128)(2,1)S(1)}, u32[]{:S(2)}, u32[]{:S(2)}) collective-permute-start(bf16[1024,16]{0,1:T(8,128)(2,1)S(1)} %copy-done.3), channel_id=1, source_target_pairs={{0,80},{8,88},{16,96},{24,104},{32,112},{40,120},{48,0},{56,8},{64... | collective-permute-start | bytes 98312 | tf_op jit(solution)/shard_map/ppermute | solution.py:34
  64.4 4.3 %collective-permute-start.6 = (bf16[1024,16]{0,1:T(8,128)(2,1)S(1)}, bf16[1024,16]{0,1:T(8,128)(2,1)S(1)}, u32[]{:S(2)}, u32[]{:S(2)}) collective-permute-start(bf16[1024,16]{0,1:T(8,128)(2,1)S(1)} %copy-done.3), channel_id=1, source_target_pairs={{0,72},{8,80},{16,88},{24,96},{32,104},{40,112},{48,120},{56,0},{6... | collective-permute-start | bytes 98312 | tf_op jit(solution)/shard_map/ppermute | solution.py:34
  68.7 9.4 %collective-permute-start.7 = (bf16[1024,16]{0,1:T(8,128)(2,1)S(1)}, bf16[1024,16]{0,1:T(8,128)(2,1)S(1)}, u32[]{:S(2)}, u32[]{:S(2)}) collective-permute-start(bf16[1024,16]{0,1:T(8,128)(2,1)S(1)} %copy-done.3), channel_id=1, source_target_pairs={{0,64},{8,72},{16,80},{24,88},{32,96},{40,104},{48,112},{56,120},{... | collective-permute-start | bytes 98312 | tf_op jit(solution)/shard_map/ppermute | solution.py:34
  78.1 3.1 %collective-permute-start.8 = (bf16[1024,16]{0,1:T(8,128)(2,1)S(1)}, bf16[1024,16]{0,1:T(8,128)(2,1)S(1)}, u32[]{:S(2)}, u32[]{:S(2)}) collective-permute-start(bf16[1024,16]{0,1:T(8,128)(2,1)S(1)} %copy-done.3), channel_id=1, source_target_pairs={{0,56},{8,64},{16,72},{24,80},{32,88},{40,96},{48,104},{56,112},{6... | collective-permute-start | bytes 98312 | tf_op jit(solution)/shard_map/ppermute | solution.py:34
  81.2 10.3 %collective-permute-start.9 = (bf16[1024,16]{0,1:T(8,128)(2,1)S(1)}, bf16[1024,16]{0,1:T(8,128)(2,1)S(1)}, u32[]{:S(2)}, u32[]{:S(2)}) collective-permute-start(bf16[1024,16]{0,1:T(8,128)(2,1)S(1)} %copy-done.3), channel_id=1, source_target_pairs={{0,48},{8,56},{16,64},{24,72},{32,80},{40,88},{48,96},{56,104},{64... | collective-permute-start | bytes 98312 | tf_op jit(solution)/shard_map/ppermute | solution.py:34
  91.5 6.7 %collective-permute-start.10 = (bf16[1024,16]{0,1:T(8,128)(2,1)S(1)}, bf16[1024,16]{0,1:T(8,128)(2,1)S(1)}, u32[]{:S(2)}, u32[]{:S(2)}) collective-permute-start(bf16[1024,16]{0,1:T(8,128)(2,1)S(1)} %copy-done.3), channel_id=1, source_target_pairs={{0,40},{8,48},{16,56},{24,64},{32,72},{40,80},{48,88},{56,96},{64,... | collective-permute-start | bytes 98312 | tf_op jit(solution)/shard_map/ppermute | solution.py:34
  98.2 1.9 collective-permute-start.11
  100.2 5.2 %collective-permute-start.12 = (bf16[1024,16]{0,1:T(8,128)(2,1)S(1)}, bf16[1024,16]{0,1:T(8,128)(2,1)S(1)}, u32[]{:S(2)}, u32[]{:S(2)}) collective-permute-start(bf16[1024,16]{0,1:T(8,128)(2,1)S(1)} %copy-done.3), channel_id=1, source_target_pairs={{0,24},{8,32},{16,40},{24,48},{32,56},{40,64},{48,72},{56,80},{64,... | collective-permute-start | bytes 98312 | tf_op jit(solution)/shard_map/ppermute | solution.py:34
  105.5 2.7 %collective-permute-start.13 = (bf16[1024,16]{0,1:T(8,128)(2,1)S(1)}, bf16[1024,16]{0,1:T(8,128)(2,1)S(1)}, u32[]{:S(2)}, u32[]{:S(2)}) collective-permute-start(bf16[1024,16]{0,1:T(8,128)(2,1)S(1)} %copy-done.3), channel_id=1, source_target_pairs={{0,16},{8,24},{16,32},{24,40},{32,48},{40,56},{48,64},{56,72},{64,... | collective-permute-start | bytes 98312 | tf_op jit(solution)/shard_map/ppermute | solution.py:34
  108.1 4.8 %collective-permute-start.14 = (bf16[1024,16]{0,1:T(8,128)(2,1)S(1)}, bf16[1024,16]{0,1:T(8,128)(2,1)S(1)}, u32[]{:S(2)}, u32[]{:S(2)}) collective-permute-start(bf16[1024,16]{0,1:T(8,128)(2,1)S(1)} %copy-done.3), channel_id=1, source_target_pairs={{0,8},{8,16},{16,24},{24,32},{32,40},{40,48},{48,56},{56,64},{64,7... | collective-permute-start | bytes 98312 | tf_op jit(solution)/shard_map/ppermute | solution.py:34
  113.4 1.8 collective-permute-done.14
  115.4 4.8 %collective-permute-start.15 = (bf16[1024,256]{0,1:T(8,128)(2,1)S(1)}, bf16[1024,256]{0,1:T(8,128)(2,1)S(1)}, u32[]{:S(2)}, u32[]{:S(2)}) collective-permute-start(bf16[1024,256]{0,1:T(8,128)(2,1)S(1)} %bitcast.143), channel_id=1, source_target_pairs={{0,384},{128,0},{256,128},{384,256},{1,385},{129,1},{257,129},{385... | collective-permute-start | bytes 1572872 | tf_op jit(solution)/shard_map/ppermute | solution.py:34
  120.3 2.5 collective-permute-start.16
  123.0 2.9 %collective-permute-start.17 = (bf16[1024,256]{0,1:T(8,128)(2,1)S(1)}, bf16[1024,256]{0,1:T(8,128)(2,1)S(1)}, u32[]{:S(2)}, u32[]{:S(2)}) collective-permute-start(bf16[1024,256]{0,1:T(8,128)(2,1)S(1)} %bitcast.145), channel_id=1, source_target_pairs={{0,128},{128,256},{256,384},{384,0},{1,129},{129,257},{257,385},{3... | collective-permute-start | bytes 1572872 | tf_op jit(solution)/shard_map/ppermute | solution.py:34
  125.9 11.5 %collective-permute-done.15 = bf16[1024,256]{0,1:T(8,128)(2,1)S(1)} collective-permute-done((bf16[1024,256]{0,1:T(8,128)(2,1)S(1)}, bf16[1024,256]{0,1:T(8,128)(2,1)S(1)}, u32[]{:S(2)}, u32[]{:S(2)}) %collective-permute-start.15) | collective-permute-done | bytes 524320 | tf_op jit(solution)/shard_map/ppermute | solution.py:34
  137.6 5.5 %collective-permute-done.17 = bf16[1024,256]{0,1:T(8,128)(2,1)S(1)} collective-permute-done((bf16[1024,256]{0,1:T(8,128)(2,1)S(1)}, bf16[1024,256]{0,1:T(8,128)(2,1)S(1)}, u32[]{:S(2)}, u32[]{:S(2)}) %collective-permute-start.17) | collective-permute-done | bytes 524320 | tf_op jit(solution)/shard_map/ppermute | solution.py:34
  146.4 22.7 %all-reduce.2 = (bf16[3,128,64]{1,2,0:T(8,128)(2,1)S(1)}, bf16[3,128,64]{1,2,0:T(8,128)(2,1)S(1)}) all-reduce(f32[3,128,64]{1,2,0:T(8,128)S(1)} %convolution_bitcast_fusion.2, f32[3,128,64]{1,2,0:T(8,128)S(1)} %convolution_multiply_fusion.2), channel_id=1, replica_groups=mesh['ay'=4,'az'=16,'mp'=8] {'mp'}, use_global_device_ids=true, to_apply=%region_2.3 | all-reduce | flops 49152 | bytes 294912 | tf_op jit(solution)/shard_map/psum | solution.py:105
  176.1 10.2 %all-to-all-start.1 = ((f32[3,64,1152]{2,0,1:T(4,128)}), f32[3,64,1152]{2,0,1:T(4,128)S(1)}, u32[]{:S(2)}, u32[]{:S(2)}) async-start(f32[3,64,1152]{2,0,1:T(4,128)} %copy.83), calls=%async_computation.2 | async-start | bytes 2359296 | tf_op jit(solution)/shard_map/all_to_all | solution.py:134
  186.4 4.0 %convolution_bitcast_fusion = f32[384,1024]{0,1:T(8,128)} fusion(bf16[1024,1024]{0,1:T(8,128)(2,1)} %bitcast.150, bf16[384,1024]{1,0:T(8,128)(2,1)S(1)} %copy-done), kind=kOutput, calls=%fused_computation.4 | convolution fusion | flops 805306368 | bytes 4456448 | tf_op jit(solution)/shard_map/dot_general | solution.py:100
  190.4 15.3 %all_gather.3 = bf16[384,1024]{1,0:T(8,128)(2,1)} all-gather(bf16[384,128]{1,0:T(8,128)(2,1)S(1)} %broadcast_multiply_fusion), channel_id=1, replica_groups=mesh['ay'=4,'az'=16,'mp'=8] {'mp'}, dimensions={1}, use_global_device_ids=true | all-gather | bytes 884736 | tf_op jit(solution)/shard_map/all_gather | solution.py:82
  206.5 3.7 %fusion = bf16[384,1024]{1,0:T(8,128)(2,1)} fusion(f32[3,128,1024]{2,1,0:T(8,128)S(1)} %fusion.19, bf16[384,1024]{1,0:T(8,128)(2,1)} %all_gather.3, bf16[1024,1024]{0,1:T(8,128)(2,1)} %bitcast.151), kind=kOutput, calls=%fused_computation.3 | convolution fusion | flops 806092800 | bytes 5242880 | tf_op jit(solution)/shard_map/dot_general | solution.py:118
  210.2 19.9 %reduce-scatter.2.cloned.1.call-done = f32[384,128]{0,1:T(8,128)} async-done(((f32[384,1024]{0,1:T(8,128)}), f32[384,128]{0,1:T(8,128)}) %reduce-scatter.2.cloned.1.call-update) | async-done | bytes 196624 | tf_op jit(solution)/shard_map/reduce_scatter | solution.py:101
  231.8 14.7 %all-to-all-done.1 = f32[3,64,1152]{2,0,1:T(4,128)S(1)} async-done(((f32[3,64,1152]{2,0,1:T(4,128)}), f32[3,64,1152]{2,0,1:T(4,128)S(1)}, u32[]{:S(2)}, u32[]{:S(2)}) %all-to-all-start.1) | async-done | bytes 884768 | tf_op jit(solution)/shard_map/all_to_all | solution.py:134
  246.5 2.1 all_to_all.21
  248.6 1.7 slice.22
  251.3 2.6 divide_subtract_fusion
  (109 shorter events, 21.9 us)
Async XLA Ops:
  7.2 138.8 %copy-start = (bf16[384,1024]{1,0:T(8,128)(2,1)S(1)}, bf16[384,1024]{1,0:T(8,128)(2,1)}, u32[]{:S(2)}) copy-start(bf16[384,1024]{1,0:T(8,128)(2,1)} %param.12) | copy-start | bytes 2359300
  7.2 46.7 %copy-start.3 = (bf16[1024,16]{0,1:T(8,128)(2,1)S(1)}, bf16[1024,16]{0,1:T(8,128)(2,1)}, u32[]{:S(2)}) copy-start(bf16[1024,16]{0,1:T(8,128)(2,1)} %param.14) | copy-start | bytes 98308
  7.2 46.7 %copy-start.7 = (s32[192]{0:T(256)S(1)}, s32[192]{0:T(256)}, u32[]{:S(2)}) copy-start(s32[192]{0:T(256)} %param.22) | copy-start | bytes 2308
  7.2 46.8 %collective-permute-start = (bf16[1024,16]{0,1:T(8,128)(2,1)}, bf16[1024,16]{0,1:T(8,128)(2,1)S(1)}, u32[]{:S(2)}, u32[]{:S(2)}) collective-permute-start(bf16[1024,16]{0,1:T(8,128)(2,1)} %param.14), channel_id=1, source_target_pairs={{0,120},{8,0},{16,8},{24,16},{32,24},{40,32},{48,40},{56,48},{64,5... | collective-permute-start | bytes 98312 | tf_op jit(solution)/shard_map/ppermute | solution.py:34
  18.7 45.6 %collective-permute-start.1 = (bf16[1024,16]{0,1:T(8,128)(2,1)}, bf16[1024,16]{0,1:T(8,128)(2,1)S(1)}, u32[]{:S(2)}, u32[]{:S(2)}) collective-permute-start(bf16[1024,16]{0,1:T(8,128)(2,1)} %param.14), channel_id=1, source_target_pairs={{0,112},{8,120},{16,0},{24,8},{32,16},{40,24},{48,32},{56,40},{64,... | collective-permute-start | bytes 98312 | tf_op jit(solution)/shard_map/ppermute | solution.py:34
  22.1 46.6 %collective-permute-start.2 = (bf16[1024,16]{0,1:T(8,128)(2,1)}, bf16[1024,16]{0,1:T(8,128)(2,1)S(1)}, u32[]{:S(2)}, u32[]{:S(2)}) collective-permute-start(bf16[1024,16]{0,1:T(8,128)(2,1)} %param.14), channel_id=1, source_target_pairs={{0,104},{8,112},{16,120},{24,0},{32,8},{40,16},{48,24},{56,32},{64... | collective-permute-start | bytes 98312 | tf_op jit(solution)/shard_map/ppermute | solution.py:34
  27.1 51.0 %collective-permute-start.3 = (bf16[1024,16]{0,1:T(8,128)(2,1)}, bf16[1024,16]{0,1:T(8,128)(2,1)S(1)}, u32[]{:S(2)}, u32[]{:S(2)}) collective-permute-start(bf16[1024,16]{0,1:T(8,128)(2,1)} %param.14), channel_id=1, source_target_pairs={{0,96},{8,104},{16,112},{24,120},{32,0},{40,8},{48,16},{56,24},{64... | collective-permute-start | bytes 98312 | tf_op jit(solution)/shard_map/ppermute | solution.py:34
  30.0 51.2 %collective-permute-start.4 = (bf16[1024,16]{0,1:T(8,128)(2,1)}, bf16[1024,16]{0,1:T(8,128)(2,1)S(1)}, u32[]{:S(2)}, u32[]{:S(2)}) collective-permute-start(bf16[1024,16]{0,1:T(8,128)(2,1)} %param.14), channel_id=1, source_target_pairs={{0,88},{8,96},{16,104},{24,112},{32,120},{40,0},{48,8},{56,16},{64... | collective-permute-start | bytes 98312 | tf_op jit(solution)/shard_map/ppermute | solution.py:34
  34.2 88.7 %copy-start.4 = (bf16[384,128]{1,0:T(8,128)(2,1)S(1)}, bf16[384,128]{1,0:T(8,128)(2,1)}, u32[]{:S(2)}) copy-start(bf16[384,128]{1,0:T(8,128)(2,1)} %param.13) | copy-start | bytes 294916
  38.1 106.8 %all-to-all-start = ((bf16[64,3,1152]{2,1,0:T(4,128)(2,1)}), bf16[64,3,1152]{2,1,0:T(4,128)(2,1)S(1)}, u32[]{:S(2)}, u32[]{:S(2)}) async-start(bf16[64,3,1152]{2,1,0:T(4,128)(2,1)} %pad_maximum_fusion.1), calls=%async_computation.1 | async-start | bytes 1179648 | tf_op jit(solution)/shard_map/all_to_all | solution.py:89
  54.0 37.5 %collective-permute-start.5 = (bf16[1024,16]{0,1:T(8,128)(2,1)S(1)}, bf16[1024,16]{0,1:T(8,128)(2,1)S(1)}, u32[]{:S(2)}, u32[]{:S(2)}) collective-permute-start(bf16[1024,16]{0,1:T(8,128)(2,1)S(1)} %copy-done.3), channel_id=1, source_target_pairs={{0,80},{8,88},{16,96},{24,104},{32,112},{40,120},{48,0},{56,8},{64... | collective-permute-start | bytes 98312 | tf_op jit(solution)/shard_map/ppermute | solution.py:34
  64.4 33.8 %collective-permute-start.6 = (bf16[1024,16]{0,1:T(8,128)(2,1)S(1)}, bf16[1024,16]{0,1:T(8,128)(2,1)S(1)}, u32[]{:S(2)}, u32[]{:S(2)}) collective-permute-start(bf16[1024,16]{0,1:T(8,128)(2,1)S(1)} %copy-done.3), channel_id=1, source_target_pairs={{0,72},{8,80},{16,88},{24,96},{32,104},{40,112},{48,120},{56,0},{6... | collective-permute-start | bytes 98312 | tf_op jit(solution)/shard_map/ppermute | solution.py:34
  68.7 31.5 %collective-permute-start.7 = (bf16[1024,16]{0,1:T(8,128)(2,1)S(1)}, bf16[1024,16]{0,1:T(8,128)(2,1)S(1)}, u32[]{:S(2)}, u32[]{:S(2)}) collective-permute-start(bf16[1024,16]{0,1:T(8,128)(2,1)S(1)} %copy-done.3), channel_id=1, source_target_pairs={{0,64},{8,72},{16,80},{24,88},{32,96},{40,104},{48,112},{56,120},{... | collective-permute-start | bytes 98312 | tf_op jit(solution)/shard_map/ppermute | solution.py:34
  78.1 27.3 %collective-permute-start.8 = (bf16[1024,16]{0,1:T(8,128)(2,1)S(1)}, bf16[1024,16]{0,1:T(8,128)(2,1)S(1)}, u32[]{:S(2)}, u32[]{:S(2)}) collective-permute-start(bf16[1024,16]{0,1:T(8,128)(2,1)S(1)} %copy-done.3), channel_id=1, source_target_pairs={{0,56},{8,64},{16,72},{24,80},{32,88},{40,96},{48,104},{56,112},{6... | collective-permute-start | bytes 98312 | tf_op jit(solution)/shard_map/ppermute | solution.py:34
  81.2 26.9 %collective-permute-start.9 = (bf16[1024,16]{0,1:T(8,128)(2,1)S(1)}, bf16[1024,16]{0,1:T(8,128)(2,1)S(1)}, u32[]{:S(2)}, u32[]{:S(2)}) collective-permute-start(bf16[1024,16]{0,1:T(8,128)(2,1)S(1)} %copy-done.3), channel_id=1, source_target_pairs={{0,48},{8,56},{16,64},{24,72},{32,80},{40,88},{48,96},{56,104},{64... | collective-permute-start | bytes 98312 | tf_op jit(solution)/shard_map/ppermute | solution.py:34
  91.5 21.4 %collective-permute-start.10 = (bf16[1024,16]{0,1:T(8,128)(2,1)S(1)}, bf16[1024,16]{0,1:T(8,128)(2,1)S(1)}, u32[]{:S(2)}, u32[]{:S(2)}) collective-permute-start(bf16[1024,16]{0,1:T(8,128)(2,1)S(1)} %copy-done.3), channel_id=1, source_target_pairs={{0,40},{8,48},{16,56},{24,64},{32,72},{40,80},{48,88},{56,96},{64,... | collective-permute-start | bytes 98312 | tf_op jit(solution)/shard_map/ppermute | solution.py:34
  98.2 14.7 %collective-permute-start.11 = (bf16[1024,16]{0,1:T(8,128)(2,1)S(1)}, bf16[1024,16]{0,1:T(8,128)(2,1)S(1)}, u32[]{:S(2)}, u32[]{:S(2)}) collective-permute-start(bf16[1024,16]{0,1:T(8,128)(2,1)S(1)} %copy-done.3), channel_id=1, source_target_pairs={{0,32},{8,40},{16,48},{24,56},{32,64},{40,72},{48,80},{56,88},{64,... | collective-permute-start | bytes 98312 | tf_op jit(solution)/shard_map/ppermute | solution.py:34
  100.2 12.8 %collective-permute-start.12 = (bf16[1024,16]{0,1:T(8,128)(2,1)S(1)}, bf16[1024,16]{0,1:T(8,128)(2,1)S(1)}, u32[]{:S(2)}, u32[]{:S(2)}) collective-permute-start(bf16[1024,16]{0,1:T(8,128)(2,1)S(1)} %copy-done.3), channel_id=1, source_target_pairs={{0,24},{8,32},{16,40},{24,48},{32,56},{40,64},{48,72},{56,80},{64,... | collective-permute-start | bytes 98312 | tf_op jit(solution)/shard_map/ppermute | solution.py:34
  105.5 7.9 %collective-permute-start.13 = (bf16[1024,16]{0,1:T(8,128)(2,1)S(1)}, bf16[1024,16]{0,1:T(8,128)(2,1)S(1)}, u32[]{:S(2)}, u32[]{:S(2)}) collective-permute-start(bf16[1024,16]{0,1:T(8,128)(2,1)S(1)} %copy-done.3), channel_id=1, source_target_pairs={{0,16},{8,24},{16,32},{24,40},{32,48},{40,56},{48,64},{56,72},{64,... | collective-permute-start | bytes 98312 | tf_op jit(solution)/shard_map/ppermute | solution.py:34
  108.1 7.0 %collective-permute-start.14 = (bf16[1024,16]{0,1:T(8,128)(2,1)S(1)}, bf16[1024,16]{0,1:T(8,128)(2,1)S(1)}, u32[]{:S(2)}, u32[]{:S(2)}) collective-permute-start(bf16[1024,16]{0,1:T(8,128)(2,1)S(1)} %copy-done.3), channel_id=1, source_target_pairs={{0,8},{8,16},{16,24},{24,32},{32,40},{40,48},{48,56},{56,64},{64,7... | collective-permute-start | bytes 98312 | tf_op jit(solution)/shard_map/ppermute | solution.py:34
  115.4 22.0 %collective-permute-start.15 = (bf16[1024,256]{0,1:T(8,128)(2,1)S(1)}, bf16[1024,256]{0,1:T(8,128)(2,1)S(1)}, u32[]{:S(2)}, u32[]{:S(2)}) collective-permute-start(bf16[1024,256]{0,1:T(8,128)(2,1)S(1)} %bitcast.143), channel_id=1, source_target_pairs={{0,384},{128,0},{256,128},{384,256},{1,385},{129,1},{257,129},{385... | collective-permute-start | bytes 1572872 | tf_op jit(solution)/shard_map/ppermute | solution.py:34
  120.3 17.2 %collective-permute-start.16 = (bf16[1024,256]{0,1:T(8,128)(2,1)S(1)}, bf16[1024,256]{0,1:T(8,128)(2,1)S(1)}, u32[]{:S(2)}, u32[]{:S(2)}) collective-permute-start(bf16[1024,256]{0,1:T(8,128)(2,1)S(1)} %bitcast.144), channel_id=1, source_target_pairs={{0,256},{128,384},{256,0},{384,128},{1,257},{129,385},{257,1},{385... | collective-permute-start | bytes 1572872 | tf_op jit(solution)/shard_map/ppermute | solution.py:34
  123.0 20.1 %collective-permute-start.17 = (bf16[1024,256]{0,1:T(8,128)(2,1)S(1)}, bf16[1024,256]{0,1:T(8,128)(2,1)S(1)}, u32[]{:S(2)}, u32[]{:S(2)}) collective-permute-start(bf16[1024,256]{0,1:T(8,128)(2,1)S(1)} %bitcast.145), channel_id=1, source_target_pairs={{0,128},{128,256},{256,384},{384,0},{1,129},{129,257},{257,385},{3... | collective-permute-start | bytes 1572872 | tf_op jit(solution)/shard_map/ppermute | solution.py:34
  176.1 70.4 %all-to-all-start.1 = ((f32[3,64,1152]{2,0,1:T(4,128)}), f32[3,64,1152]{2,0,1:T(4,128)S(1)}, u32[]{:S(2)}, u32[]{:S(2)}) async-start(f32[3,64,1152]{2,0,1:T(4,128)} %copy.83), calls=%async_computation.2 | async-start | bytes 2359296 | tf_op jit(solution)/shard_map/all_to_all | solution.py:134
  186.3 43.7 %reduce-scatter.2.cloned.1.call-start = ((), (), s32[]{:S(2)}) async-start(), calls=%async_computation.3 | async-start | bytes 1769472 | tf_op jit(solution)/shard_map/reduce_scatter | solution.py:101
  210.2 41.1 %copy-start.2 = (bf16[128,1,16,64]{0,3,2,1:T(8,128)(2,1)S(1)}, bf16[128,1,16,64]{0,3,2,1:T(8,128)(2,1)}, u32[]{:S(2)}) copy-start(bf16[128,1,16,64]{0,3,2,1:T(8,128)(2,1)} %param.15) | copy-start | bytes 786436
  246.5 7.4 %copy-start.1 = (bf16[128,1,128]{2,0,1:T(8,128)(2,1)S(1)}, bf16[128,1,128]{2,0,1:T(8,128)(2,1)}, u32[]{:S(2)}) copy-start(bf16[128,1,128]{2,0,1:T(8,128)(2,1)} %param.18) | copy-start | bytes 98308
  246.5 7.4 %copy-start.5 = (f32[128,1,128]{2,1,0:T(1,128)S(1)}, f32[128,1,128]{2,1,0:T(1,128)}, u32[]{:S(2)}) copy-start(f32[128,1,128]{2,1,0:T(1,128)} %param.19) | copy-start | bytes 196612
  246.5 7.4 %copy-start.6 = (f32[128,1,128]{2,1,0:T(1,128)S(1)}, f32[128,1,128]{2,1,0:T(1,128)}, u32[]{:S(2)}) copy-start(f32[128,1,128]{2,1,0:T(1,128)} %param.20) | copy-start | bytes 196612
  248.6 5.4 %slice-start = ((f32[192,1,1152]{2,1,0:T(1,128)}), f32[192,1,128]{2,1,0:T(1,128)S(1)}, s32[]{:S(2)}) async-start(f32[192,1,1152]{2,1,0:T(1,128)} %all_to_all.21), calls=%async_computation.4 | async-start | bytes 196608 | tf_op jit(solution)/shard_map/slice | solution.py:136
Sparse Core Ops, SparseCore 0:
  190.5 39.4 reduce-scatter.1
where the time goes:
time: 263 us; the launch traced here: 262 us
  starting transfers between devices  120 us (46%)
  waiting for transfers between devices  54 us (21%)
  blocking collectives  38 us (14%)
  local copies, waits for them, and re-layouts  16.4 us (6%)
  between operations  14.8 us (6%)
  matrix products  12.2 us (5%)
  other arithmetic  6.9 us (3%)
    ppermute x18, starting transfers between devices, gather_along(): got.append(lax.ppermute(piece, axis, pairs))  93.5 us
    psum x1, blocking collectives, shards(): down_sum = lax.psum(down_part, 'mp')  22.7 us
    reduce_scatter x1, waiting for transfers between devices, shards(): lax.psum_scatter(frozen_part, 'mp', scatter_dimension=1, tiled=True)  19.9 us
    ppermute x18, waiting for transfers between devices, gather_along(): got.append(lax.ppermute(piece, axis, pairs))  19.3 us
    all_to_all x1, starting transfers between devices, shards(): lax.all_to_all(sent, ADAPTER, split_axis=0, concat_axis=0, tiled=True)  15.8 us
    all_gather x1, blocking collectives, shards(): masked_full = lax.all_gather(masked_own, 'mp', axis=1, tiled=True)  15.3 us
    all_to_all x1, waiting for transfers between devices, shards(): lax.all_to_all(grads, ADAPTER, split_axis=1, concat_axis=0, tiled=True)  14.7 us
    all_to_all x1, starting transfers between devices, shards(): lax.all_to_all(grads, ADAPTER, split_axis=1, concat_axis=0, tiled=True)  10.2 us
  transfers between devices with their start and end apart: 21, of which 7 were waited for; matrix products, arithmetic and copies ran while one was open for 7% of the time, Pallas kernels for 0%

commit v1 on v0

--- a/solution.py
+++ b/solution.py
@@ -102,7 +102,11 @@
     down_part = jnp.einsum(
         "ntd,ndr->ntr", token_tiles, down_panel, preferred_element_type=jnp.float32
     )
-    down_sum = lax.psum(down_part, "mp")
+
+    def panels_convert(target):
+        return jnp.sum(lax.all_gather(target, axis_name="mp"), 0)
+
+    down_sum = panels_convert(down_part)
     down_portion = down_sum.astype(jnp.bfloat16)
     adapter_term = jnp.einsum(
         "ntr,nrv->ntv", down_portion, up_panel, preferred_element_type=jnp.float32

time: 263 us -> 280 us (1.065)
  blocking collectives: 38 us -> 50.8 us
    all_gather x0 -> x1, blocking collectives: none -> 15.1 us  [panels_convert(): return jnp.sum(lax.all_gather(target, axis_name='mp'), 0)]
where the time goes in v1:
time: 280 us; the launch traced here: 277 us
  starting transfers between devices  120 us (43%)
  waiting for transfers between devices  55 us (20%)
  blocking collectives  50.8 us (18%)
  local copies, waits for them, and re-layouts  16.3 us (6%)
  between operations  14.8 us (5%)
  matrix products  12.2 us (4%)
  other arithmetic  8.09 us (3%)
    ppermute x18, starting transfers between devices, gather_along(): got.append(lax.ppermute(piece, axis, pairs))  93.5 us
    psum x1, blocking collectives, shards(): backward_portion = lax.psum(backward_piece, 'mp').astype(jnp.bfloat16)  21.6 us
    reduce_scatter x1, waiting for transfers between devices, shards(): lax.psum_scatter(frozen_part, 'mp', scatter_dimension=1, tiled=True)  21.2 us
    ppermute x18, waiting for transfers between devices, gather_along(): got.append(lax.ppermute(piece, axis, pairs))  19.3 us
    all_to_all x1, starting transfers between devices, shards(): lax.all_to_all(sent, ADAPTER, split_axis=0, concat_axis=0, tiled=True)  15.8 us
    all_gather x1, blocking collectives, panels_convert(): return jnp.sum(lax.all_gather(target, axis_name='mp'), 0)  15.1 us
    all_to_all x1, waiting for transfers between devices, shards(): lax.all_to_all(grads, ADAPTER, split_axis=1, concat_axis=0, tiled=True)  14.5 us
    all_gather x1, blocking collectives, shards(): masked_full = lax.all_gather(masked_own, 'mp', axis=1, tiled=True)  14.2 us
  transfers between devices with their start and end apart: 21, of which 7 were waited for; matrix products, arithmetic and copies ran while one was open for 7% of the time, Pallas kernels for 0%

profile of v1, /device:TPU:6, one launch (start us, length us, event | category | flops | bytes accessed | tf_op | source)
XLA Modules:
  0.0 276.7 jit_solution(7047835618206040679)
XLA Ops:
  7.2 11.5 %collective-permute-start = (bf16[1024,16]{0,1:T(8,128)(2,1)}, bf16[1024,16]{0,1:T(8,128)(2,1)S(1)}, u32[]{:S(2)}, u32[]{:S(2)}) collective-permute-start(bf16[1024,16]{0,1:T(8,128)(2,1)} %param.14), channel_id=1, source_target_pairs={{0,120},{8,0},{16,8},{24,16},{32,24},{40,32},{48,40},{56,48},{64,5... | collective-permute-start | bytes 98312 | tf_op jit(solution)/shard_map/ppermute | solution.py:34
  18.7 3.4 %collective-permute-start.1 = (bf16[1024,16]{0,1:T(8,128)(2,1)}, bf16[1024,16]{0,1:T(8,128)(2,1)S(1)}, u32[]{:S(2)}, u32[]{:S(2)}) collective-permute-start(bf16[1024,16]{0,1:T(8,128)(2,1)} %param.14), channel_id=1, source_target_pairs={{0,112},{8,120},{16,0},{24,8},{32,16},{40,24},{48,32},{56,40},{64,... | collective-permute-start | bytes 98312 | tf_op jit(solution)/shard_map/ppermute | solution.py:34
  22.1 5.0 %collective-permute-start.2 = (bf16[1024,16]{0,1:T(8,128)(2,1)}, bf16[1024,16]{0,1:T(8,128)(2,1)S(1)}, u32[]{:S(2)}, u32[]{:S(2)}) collective-permute-start(bf16[1024,16]{0,1:T(8,128)(2,1)} %param.14), channel_id=1, source_target_pairs={{0,104},{8,112},{16,120},{24,0},{32,8},{40,16},{48,24},{56,32},{64... | collective-permute-start | bytes 98312 | tf_op jit(solution)/shard_map/ppermute | solution.py:34
  27.1 2.8 %collective-permute-start.3 = (bf16[1024,16]{0,1:T(8,128)(2,1)}, bf16[1024,16]{0,1:T(8,128)(2,1)S(1)}, u32[]{:S(2)}, u32[]{:S(2)}) collective-permute-start(bf16[1024,16]{0,1:T(8,128)(2,1)} %param.14), channel_id=1, source_target_pairs={{0,96},{8,104},{16,112},{24,120},{32,0},{40,8},{48,16},{56,24},{64... | collective-permute-start | bytes 98312 | tf_op jit(solution)/shard_map/ppermute | solution.py:34
  30.0 1.9 collective-permute-start.4
  38.1 15.8 %all-to-all-start = ((bf16[64,3,1152]{2,1,0:T(4,128)(2,1)}), bf16[64,3,1152]{2,1,0:T(4,128)(2,1)S(1)}, u32[]{:S(2)}, u32[]{:S(2)}) async-start(bf16[64,3,1152]{2,1,0:T(4,128)(2,1)} %pad_maximum_fusion.1), calls=%async_computation.1 | async-start | bytes 1179648 | tf_op jit(solution)/shard_map/all_to_all | solution.py:89
  54.0 10.4 %collective-permute-start.5 = (bf16[1024,16]{0,1:T(8,128)(2,1)S(1)}, bf16[1024,16]{0,1:T(8,128)(2,1)S(1)}, u32[]{:S(2)}, u32[]{:S(2)}) collective-permute-start(bf16[1024,16]{0,1:T(8,128)(2,1)S(1)} %copy-done.3), channel_id=1, source_target_pairs={{0,80},{8,88},{16,96},{24,104},{32,112},{40,120},{48,0},{56,8},{64... | collective-permute-start | bytes 98312 | tf_op jit(solution)/shard_map/ppermute | solution.py:34
  64.4 4.3 %collective-permute-start.6 = (bf16[1024,16]{0,1:T(8,128)(2,1)S(1)}, bf16[1024,16]{0,1:T(8,128)(2,1)S(1)}, u32[]{:S(2)}, u32[]{:S(2)}) collective-permute-start(bf16[1024,16]{0,1:T(8,128)(2,1)S(1)} %copy-done.3), channel_id=1, source_target_pairs={{0,72},{8,80},{16,88},{24,96},{32,104},{40,112},{48,120},{56,0},{6... | collective-permute-start | bytes 98312 | tf_op jit(solution)/shard_map/ppermute | solution.py:34
  68.7 9.4 %collective-permute-start.7 = (bf16[1024,16]{0,1:T(8,128)(2,1)S(1)}, bf16[1024,16]{0,1:T(8,128)(2,1)S(1)}, u32[]{:S(2)}, u32[]{:S(2)}) collective-permute-start(bf16[1024,16]{0,1:T(8,128)(2,1)S(1)} %copy-done.3), channel_id=1, source_target_pairs={{0,64},{8,72},{16,80},{24,88},{32,96},{40,104},{48,112},{56,120},{... | collective-permute-start | bytes 98312 | tf_op jit(solution)/shard_map/ppermute | solution.py:34
  78.1 3.1 %collective-permute-start.8 = (bf16[1024,16]{0,1:T(8,128)(2,1)S(1)}, bf16[1024,16]{0,1:T(8,128)(2,1)S(1)}, u32[]{:S(2)}, u32[]{:S(2)}) collective-permute-start(bf16[1024,16]{0,1:T(8,128)(2,1)S(1)} %copy-done.3), channel_id=1, source_target_pairs={{0,56},{8,64},{16,72},{24,80},{32,88},{40,96},{48,104},{56,112},{6... | collective-permute-start | bytes 98312 | tf_op jit(solution)/shard_map/ppermute | solution.py:34
  81.2 10.3 %collective-permute-start.9 = (bf16[1024,16]{0,1:T(8,128)(2,1)S(1)}, bf16[1024,16]{0,1:T(8,128)(2,1)S(1)}, u32[]{:S(2)}, u32[]{:S(2)}) collective-permute-start(bf16[1024,16]{0,1:T(8,128)(2,1)S(1)} %copy-done.3), channel_id=1, source_target_pairs={{0,48},{8,56},{16,64},{24,72},{32,80},{40,88},{48,96},{56,104},{64... | collective-permute-start | bytes 98312 | tf_op jit(solution)/shard_map/ppermute | solution.py:34
  91.5 6.7 %collective-permute-start.10 = (bf16[1024,16]{0,1:T(8,128)(2,1)S(1)}, bf16[1024,16]{0,1:T(8,128)(2,1)S(1)}, u32[]{:S(2)}, u32[]{:S(2)}) collective-permute-start(bf16[1024,16]{0,1:T(8,128)(2,1)S(1)} %copy-done.3), channel_id=1, source_target_pairs={{0,40},{8,48},{16,56},{24,64},{32,72},{40,80},{48,88},{56,96},{64,... | collective-permute-start | bytes 98312 | tf_op jit(solution)/shard_map/ppermute | solution.py:34
  98.2 1.9 collective-permute-start.11
  100.2 5.2 %collective-permute-start.12 = (bf16[1024,16]{0,1:T(8,128)(2,1)S(1)}, bf16[1024,16]{0,1:T(8,128)(2,1)S(1)}, u32[]{:S(2)}, u32[]{:S(2)}) collective-permute-start(bf16[1024,16]{0,1:T(8,128)(2,1)S(1)} %copy-done.3), channel_id=1, source_target_pairs={{0,24},{8,32},{16,40},{24,48},{32,56},{40,64},{48,72},{56,80},{64,... | collective-permute-start | bytes 98312 | tf_op jit(solution)/shard_map/ppermute | solution.py:34
  105.5 2.7 collective-permute-start.13
  108.1 4.8 %collective-permute-start.14 = (bf16[1024,16]{0,1:T(8,128)(2,1)S(1)}, bf16[1024,16]{0,1:T(8,128)(2,1)S(1)}, u32[]{:S(2)}, u32[]{:S(2)}) collective-permute-start(bf16[1024,16]{0,1:T(8,128)(2,1)S(1)} %copy-done.3), channel_id=1, source_target_pairs={{0,8},{8,16},{16,24},{24,32},{32,40},{40,48},{48,56},{56,64},{64,7... | collective-permute-start | bytes 98312 | tf_op jit(solution)/shard_map/ppermute | solution.py:34
  113.4 1.8 collective-permute-done.14
  115.4 4.8 %collective-permute-start.15 = (bf16[1024,256]{0,1:T(8,128)(2,1)S(1)}, bf16[1024,256]{0,1:T(8,128)(2,1)S(1)}, u32[]{:S(2)}, u32[]{:S(2)}) collective-permute-start(bf16[1024,256]{0,1:T(8,128)(2,1)S(1)} %bitcast.144), channel_id=1, source_target_pairs={{0,384},{128,0},{256,128},{384,256},{1,385},{129,1},{257,129},{385... | collective-permute-start | bytes 1572872 | tf_op jit(solution)/shard_map/ppermute | solution.py:34
  120.3 2.5 collective-permute-start.16
  123.0 2.9 %collective-permute-start.17 = (bf16[1024,256]{0,1:T(8,128)(2,1)S(1)}, bf16[1024,256]{0,1:T(8,128)(2,1)S(1)}, u32[]{:S(2)}, u32[]{:S(2)}) collective-permute-start(bf16[1024,256]{0,1:T(8,128)(2,1)S(1)} %bitcast.146), channel_id=1, source_target_pairs={{0,128},{128,256},{256,384},{384,0},{1,129},{129,257},{257,385},{3... | collective-permute-start | bytes 1572872 | tf_op jit(solution)/shard_map/ppermute | solution.py:34
  125.9 11.5 %collective-permute-done.15 = bf16[1024,256]{0,1:T(8,128)(2,1)S(1)} collective-permute-done((bf16[1024,256]{0,1:T(8,128)(2,1)S(1)}, bf16[1024,256]{0,1:T(8,128)(2,1)S(1)}, u32[]{:S(2)}, u32[]{:S(2)}) %collective-permute-start.15) | collective-permute-done | bytes 524320 | tf_op jit(solution)/shard_map/ppermute | solution.py:34
  137.6 5.5 %collective-permute-done.17 = bf16[1024,256]{0,1:T(8,128)(2,1)S(1)} collective-permute-done((bf16[1024,256]{0,1:T(8,128)(2,1)S(1)}, bf16[1024,256]{0,1:T(8,128)(2,1)S(1)}, u32[]{:S(2)}, u32[]{:S(2)}) %collective-permute-start.17) | collective-permute-done | bytes 524320 | tf_op jit(solution)/shard_map/ppermute | solution.py:34
  145.1 21.6 %psum.7 = bf16[3,128,64]{1,2,0:T(8,128)(2,1)S(1)} all-reduce(f32[3,128,64]{1,2,0:T(8,128)S(1)} %convolution_multiply_fusion.2), channel_id=1, replica_groups=mesh['ay'=4,'az'=16,'mp'=8] {'mp'}, use_global_device_ids=true, to_apply=%region_3.4 | all-reduce | flops 24576 | bytes 147456 | tf_op jit(solution)/shard_map/psum | solution.py:121
  167.9 15.1 %all-gather = f32[24,128,64]{1,2,0:T(8,128)} all-gather(f32[3,128,64]{1,2,0:T(8,128)S(1)} %convolution_bitcast_fusion.2), channel_id=2, replica_groups=mesh['ay'=4,'az'=16,'mp'=8] {'mp'}, dimensions={0}, use_global_device_ids=true | all-gather | bytes 884736 | tf_op jit(solution)/shard_map/all_gather | solution.py:107
  191.3 10.2 %all-to-all-start.1 = ((f32[3,64,1152]{2,0,1:T(4,128)}), f32[3,64,1152]{2,0,1:T(4,128)S(1)}, u32[]{:S(2)}, u32[]{:S(2)}) async-start(f32[3,64,1152]{2,0,1:T(4,128)} %copy.83), calls=%async_computation.2 | async-start | bytes 2359296 | tf_op jit(solution)/shard_map/all_to_all | solution.py:138
  201.5 4.0 %convolution_bitcast_fusion = f32[384,1024]{0,1:T(8,128)} fusion(bf16[1024,1024]{0,1:T(8,128)(2,1)} %bitcast.152, bf16[384,1024]{1,0:T(8,128)(2,1)S(1)} %copy-done), kind=kOutput, calls=%fused_computation.4 | convolution fusion | flops 805306368 | bytes 4456448 | tf_op jit(solution)/shard_map/dot_general | solution.py:100
  205.5 14.2 %all_gather.11 = bf16[384,1024]{1,0:T(8,128)(2,1)} all-gather(bf16[384,128]{1,0:T(8,128)(2,1)S(1)} %broadcast_multiply_fusion), channel_id=1, replica_groups=mesh['ay'=4,'az'=16,'mp'=8] {'mp'}, dimensions={1}, use_global_device_ids=true | all-gather | bytes 884736 | tf_op jit(solution)/shard_map/all_gather | solution.py:82
  220.5 3.7 %fusion = bf16[384,1024]{1,0:T(8,128)(2,1)} fusion(f32[3,128,1024]{2,1,0:T(8,128)S(1)} %fusion.19, bf16[384,1024]{1,0:T(8,128)(2,1)} %all_gather.11, bf16[1024,1024]{0,1:T(8,128)(2,1)} %bitcast.153), kind=kOutput, calls=%fused_computation.3 | convolution fusion | flops 806092800 | bytes 5242880 | tf_op jit(solution)/shard_map/dot_general | solution.py:122
  224.2 21.2 %reduce-scatter.2.cloned.1.call-done = f32[384,128]{0,1:T(8,128)} async-done(((f32[384,1024]{0,1:T(8,128)}), f32[384,128]{0,1:T(8,128)}) %reduce-scatter.2.cloned.1.call-update) | async-done | bytes 196624 | tf_op jit(solution)/shard_map/reduce_scatter | solution.py:101
  247.1 14.5 %all-to-all-done.1 = f32[3,64,1152]{2,0,1:T(4,128)S(1)} async-done(((f32[3,64,1152]{2,0,1:T(4,128)}), f32[3,64,1152]{2,0,1:T(4,128)S(1)}, u32[]{:S(2)}, u32[]{:S(2)}) %all-to-all-start.1) | async-done | bytes 884768 | tf_op jit(solution)/shard_map/all_to_all | solution.py:138
  261.5 2.0 all_to_all.21
  266.3 2.6 divide_subtract_fusion
  (111 shorter events, 24.8 us)
Async XLA Ops:
  7.2 160.3 %copy-start = (bf16[384,1024]{1,0:T(8,128)(2,1)S(1)}, bf16[384,1024]{1,0:T(8,128)(2,1)}, u32[]{:S(2)}) copy-start(bf16[384,1024]{1,0:T(8,128)(2,1)} %param.12) | copy-start | bytes 2359300
  7.2 46.7 %copy-start.3 = (bf16[1024,16]{0,1:T(8,128)(2,1)S(1)}, bf16[1024,16]{0,1:T(8,128)(2,1)}, u32[]{:S(2)}) copy-start(bf16[1024,16]{0,1:T(8,128)(2,1)} %param.14) | copy-start | bytes 98308
  7.2 46.7 %copy-start.7 = (s32[192]{0:T(256)S(1)}, s32[192]{0:T(256)}, u32[]{:S(2)}) copy-start(s32[192]{0:T(256)} %param.22) | copy-start | bytes 2308
  7.2 46.8 %collective-permute-start = (bf16[1024,16]{0,1:T(8,128)(2,1)}, bf16[1024,16]{0,1:T(8,128)(2,1)S(1)}, u32[]{:S(2)}, u32[]{:S(2)}) collective-permute-start(bf16[1024,16]{0,1:T(8,128)(2,1)} %param.14), channel_id=1, source_target_pairs={{0,120},{8,0},{16,8},{24,16},{32,24},{40,32},{48,40},{56,48},{64,5... | collective-permute-start | bytes 98312 | tf_op jit(solution)/shard_map/ppermute | solution.py:34
  18.7 45.6 %collective-permute-start.1 = (bf16[1024,16]{0,1:T(8,128)(2,1)}, bf16[1024,16]{0,1:T(8,128)(2,1)S(1)}, u32[]{:S(2)}, u32[]{:S(2)}) collective-permute-start(bf16[1024,16]{0,1:T(8,128)(2,1)} %param.14), channel_id=1, source_target_pairs={{0,112},{8,120},{16,0},{24,8},{32,16},{40,24},{48,32},{56,40},{64,... | collective-permute-start | bytes 98312 | tf_op jit(solution)/shard_map/ppermute | solution.py:34
  22.1 46.6 %collective-permute-start.2 = (bf16[1024,16]{0,1:T(8,128)(2,1)}, bf16[1024,16]{0,1:T(8,128)(2,1)S(1)}, u32[]{:S(2)}, u32[]{:S(2)}) collective-permute-start(bf16[1024,16]{0,1:T(8,128)(2,1)} %param.14), channel_id=1, source_target_pairs={{0,104},{8,112},{16,120},{24,0},{32,8},{40,16},{48,24},{56,32},{64... | collective-permute-start | bytes 98312 | tf_op jit(solution)/shard_map/ppermute | solution.py:34
  27.1 51.0 %collective-permute-start.3 = (bf16[1024,16]{0,1:T(8,128)(2,1)}, bf16[1024,16]{0,1:T(8,128)(2,1)S(1)}, u32[]{:S(2)}, u32[]{:S(2)}) collective-permute-start(bf16[1024,16]{0,1:T(8,128)(2,1)} %param.14), channel_id=1, source_target_pairs={{0,96},{8,104},{16,112},{24,120},{32,0},{40,8},{48,16},{56,24},{64... | collective-permute-start | bytes 98312 | tf_op jit(solution)/shard_map/ppermute | solution.py:34
  30.0 51.2 %collective-permute-start.4 = (bf16[1024,16]{0,1:T(8,128)(2,1)}, bf16[1024,16]{0,1:T(8,128)(2,1)S(1)}, u32[]{:S(2)}, u32[]{:S(2)}) collective-permute-start(bf16[1024,16]{0,1:T(8,128)(2,1)} %param.14), channel_id=1, source_target_pairs={{0,88},{8,96},{16,104},{24,112},{32,120},{40,0},{48,8},{56,16},{64... | collective-permute-start | bytes 98312 | tf_op jit(solution)/shard_map/ppermute | solution.py:34
  34.2 88.7 %copy-start.4 = (bf16[384,128]{1,0:T(8,128)(2,1)S(1)}, bf16[384,128]{1,0:T(8,128)(2,1)}, u32[]{:S(2)}) copy-start(bf16[384,128]{1,0:T(8,128)(2,1)} %param.13) | copy-start | bytes 294916
  38.1 106.8 %all-to-all-start = ((bf16[64,3,1152]{2,1,0:T(4,128)(2,1)}), bf16[64,3,1152]{2,1,0:T(4,128)(2,1)S(1)}, u32[]{:S(2)}, u32[]{:S(2)}) async-start(bf16[64,3,1152]{2,1,0:T(4,128)(2,1)} %pad_maximum_fusion.1), calls=%async_computation.1 | async-start | bytes 1179648 | tf_op jit(solution)/shard_map/all_to_all | solution.py:89
  54.0 37.5 %collective-permute-start.5 = (bf16[1024,16]{0,1:T(8,128)(2,1)S(1)}, bf16[1024,16]{0,1:T(8,128)(2,1)S(1)}, u32[]{:S(2)}, u32[]{:S(2)}) collective-permute-start(bf16[1024,16]{0,1:T(8,128)(2,1)S(1)} %copy-done.3), channel_id=1, source_target_pairs={{0,80},{8,88},{16,96},{24,104},{32,112},{40,120},{48,0},{56,8},{64... | collective-permute-start | bytes 98312 | tf_op jit(solution)/shard_map/ppermute | solution.py:34
  64.4 33.8 %collective-permute-start.6 = (bf16[1024,16]{0,1:T(8,128)(2,1)S(1)}, bf16[1024,16]{0,1:T(8,128)(2,1)S(1)}, u32[]{:S(2)}, u32[]{:S(2)}) collective-permute-start(bf16[1024,16]{0,1:T(8,128)(2,1)S(1)} %copy-done.3), channel_id=1, source_target_pairs={{0,72},{8,80},{16,88},{24,96},{32,104},{40,112},{48,120},{56,0},{6... | collective-permute-start | bytes 98312 | tf_op jit(solution)/shard_map/ppermute | solution.py:34
  68.7 31.5 %collective-permute-start.7 = (bf16[1024,16]{0,1:T(8,128)(2,1)S(1)}, bf16[1024,16]{0,1:T(8,128)(2,1)S(1)}, u32[]{:S(2)}, u32[]{:S(2)}) collective-permute-start(bf16[1024,16]{0,1:T(8,128)(2,1)S(1)} %copy-done.3), channel_id=1, source_target_pairs={{0,64},{8,72},{16,80},{24,88},{32,96},{40,104},{48,112},{56,120},{... | collective-permute-start | bytes 98312 | tf_op jit(solution)/shard_map/ppermute | solution.py:34
  78.1 27.3 %collective-permute-start.8 = (bf16[1024,16]{0,1:T(8,128)(2,1)S(1)}, bf16[1024,16]{0,1:T(8,128)(2,1)S(1)}, u32[]{:S(2)}, u32[]{:S(2)}) collective-permute-start(bf16[1024,16]{0,1:T(8,128)(2,1)S(1)} %copy-done.3), channel_id=1, source_target_pairs={{0,56},{8,64},{16,72},{24,80},{32,88},{40,96},{48,104},{56,112},{6... | collective-permute-start | bytes 98312 | tf_op jit(solution)/shard_map/ppermute | solution.py:34
  81.2 26.9 %collective-permute-start.9 = (bf16[1024,16]{0,1:T(8,128)(2,1)S(1)}, bf16[1024,16]{0,1:T(8,128)(2,1)S(1)}, u32[]{:S(2)}, u32[]{:S(2)}) collective-permute-start(bf16[1024,16]{0,1:T(8,128)(2,1)S(1)} %copy-done.3), channel_id=1, source_target_pairs={{0,48},{8,56},{16,64},{24,72},{32,80},{40,88},{48,96},{56,104},{64... | collective-permute-start | bytes 98312 | tf_op jit(solution)/shard_map/ppermute | solution.py:34
  91.5 21.4 %collective-permute-start.10 = (bf16[1024,16]{0,1:T(8,128)(2,1)S(1)}, bf16[1024,16]{0,1:T(8,128)(2,1)S(1)}, u32[]{:S(2)}, u32[]{:S(2)}) collective-permute-start(bf16[1024,16]{0,1:T(8,128)(2,1)S(1)} %copy-done.3), channel_id=1, source_target_pairs={{0,40},{8,48},{16,56},{24,64},{32,72},{40,80},{48,88},{56,96},{64,... | collective-permute-start | bytes 98312 | tf_op jit(solution)/shard_map/ppermute | solution.py:34
  98.2 14.7 %collective-permute-start.11 = (bf16[1024,16]{0,1:T(8,128)(2,1)S(1)}, bf16[1024,16]{0,1:T(8,128)(2,1)S(1)}, u32[]{:S(2)}, u32[]{:S(2)}) collective-permute-start(bf16[1024,16]{0,1:T(8,128)(2,1)S(1)} %copy-done.3), channel_id=1, source_target_pairs={{0,32},{8,40},{16,48},{24,56},{32,64},{40,72},{48,80},{56,88},{64,... | collective-permute-start | bytes 98312 | tf_op jit(solution)/shard_map/ppermute | solution.py:34
  100.2 12.8 %collective-permute-start.12 = (bf16[1024,16]{0,1:T(8,128)(2,1)S(1)}, bf16[1024,16]{0,1:T(8,128)(2,1)S(1)}, u32[]{:S(2)}, u32[]{:S(2)}) collective-permute-start(bf16[1024,16]{0,1:T(8,128)(2,1)S(1)} %copy-done.3), channel_id=1, source_target_pairs={{0,24},{8,32},{16,40},{24,48},{32,56},{40,64},{48,72},{56,80},{64,... | collective-permute-start | bytes 98312 | tf_op jit(solution)/shard_map/ppermute | solution.py:34
  105.5 7.9 %collective-permute-start.13 = (bf16[1024,16]{0,1:T(8,128)(2,1)S(1)}, bf16[1024,16]{0,1:T(8,128)(2,1)S(1)}, u32[]{:S(2)}, u32[]{:S(2)}) collective-permute-start(bf16[1024,16]{0,1:T(8,128)(2,1)S(1)} %copy-done.3), channel_id=1, source_target_pairs={{0,16},{8,24},{16,32},{24,40},{32,48},{40,56},{48,64},{56,72},{64,... | collective-permute-start | bytes 98312 | tf_op jit(solution)/shard_map/ppermute | solution.py:34
  108.1 7.0 %collective-permute-start.14 = (bf16[1024,16]{0,1:T(8,128)(2,1)S(1)}, bf16[1024,16]{0,1:T(8,128)(2,1)S(1)}, u32[]{:S(2)}, u32[]{:S(2)}) collective-permute-start(bf16[1024,16]{0,1:T(8,128)(2,1)S(1)} %copy-done.3), channel_id=1, source_target_pairs={{0,8},{8,16},{16,24},{24,32},{32,40},{40,48},{48,56},{56,64},{64,7... | collective-permute-start | bytes 98312 | tf_op jit(solution)/shard_map/ppermute | solution.py:34
  115.4 22.0 %collective-permute-start.15 = (bf16[1024,256]{0,1:T(8,128)(2,1)S(1)}, bf16[1024,256]{0,1:T(8,128)(2,1)S(1)}, u32[]{:S(2)}, u32[]{:S(2)}) collective-permute-start(bf16[1024,256]{0,1:T(8,128)(2,1)S(1)} %bitcast.144), channel_id=1, source_target_pairs={{0,384},{128,0},{256,128},{384,256},{1,385},{129,1},{257,129},{385... | collective-permute-start | bytes 1572872 | tf_op jit(solution)/shard_map/ppermute | solution.py:34
  120.3 17.2 %collective-permute-start.16 = (bf16[1024,256]{0,1:T(8,128)(2,1)S(1)}, bf16[1024,256]{0,1:T(8,128)(2,1)S(1)}, u32[]{:S(2)}, u32[]{:S(2)}) collective-permute-start(bf16[1024,256]{0,1:T(8,128)(2,1)S(1)} %bitcast.145), channel_id=1, source_target_pairs={{0,256},{128,384},{256,0},{384,128},{1,257},{129,385},{257,1},{385... | collective-permute-start | bytes 1572872 | tf_op jit(solution)/shard_map/ppermute | solution.py:34
  123.0 20.1 %collective-permute-start.17 = (bf16[1024,256]{0,1:T(8,128)(2,1)S(1)}, bf16[1024,256]{0,1:T(8,128)(2,1)S(1)}, u32[]{:S(2)}, u32[]{:S(2)}) collective-permute-start(bf16[1024,256]{0,1:T(8,128)(2,1)S(1)} %bitcast.146), channel_id=1, source_target_pairs={{0,128},{128,256},{256,384},{384,0},{1,129},{129,257},{257,385},{3... | collective-permute-start | bytes 1572872 | tf_op jit(solution)/shard_map/ppermute | solution.py:34
  191.3 70.3 %all-to-all-start.1 = ((f32[3,64,1152]{2,0,1:T(4,128)}), f32[3,64,1152]{2,0,1:T(4,128)S(1)}, u32[]{:S(2)}, u32[]{:S(2)}) async-start(f32[3,64,1152]{2,0,1:T(4,128)} %copy.83), calls=%async_computation.2 | async-start | bytes 2359296 | tf_op jit(solution)/shard_map/all_to_all | solution.py:138
  201.5 43.9 %reduce-scatter.2.cloned.1.call-start = ((), (), s32[]{:S(2)}) async-start(), calls=%async_computation.3 | async-start | bytes 1769472 | tf_op jit(solution)/shard_map/reduce_scatter | solution.py:101
  224.2 42.1 %copy-start.2 = (bf16[128,1,16,64]{0,3,2,1:T(8,128)(2,1)S(1)}, bf16[128,1,16,64]{0,3,2,1:T(8,128)(2,1)}, u32[]{:S(2)}) copy-start(bf16[128,1,16,64]{0,3,2,1:T(8,128)(2,1)} %param.15) | copy-start | bytes 786436
  261.5 7.4 %copy-start.1 = (bf16[128,1,128]{2,0,1:T(8,128)(2,1)S(1)}, bf16[128,1,128]{2,0,1:T(8,128)(2,1)}, u32[]{:S(2)}) copy-start(bf16[128,1,128]{2,0,1:T(8,128)(2,1)} %param.18) | copy-start | bytes 98308
  261.5 7.4 %copy-start.5 = (f32[128,1,128]{2,1,0:T(1,128)S(1)}, f32[128,1,128]{2,1,0:T(1,128)}, u32[]{:S(2)}) copy-start(f32[128,1,128]{2,1,0:T(1,128)} %param.19) | copy-start | bytes 196612
  261.5 7.4 %copy-start.6 = (f32[128,1,128]{2,1,0:T(1,128)S(1)}, f32[128,1,128]{2,1,0:T(1,128)}, u32[]{:S(2)}) copy-start(f32[128,1,128]{2,1,0:T(1,128)} %param.20) | copy-start | bytes 196612
  263.6 5.4 %slice-start = ((f32[192,1,1152]{2,1,0:T(1,128)}), f32[192,1,128]{2,1,0:T(1,128)S(1)}, s32[]{:S(2)}) async-start(f32[192,1,1152]{2,1,0:T(1,128)} %all_to_all.21), calls=%async_computation.4 | async-start | bytes 196608 | tf_op jit(solution)/shard_map/slice | solution.py:140
Sparse Core Ops, SparseCore 0:
  205.7 39.6 reduce-scatter.1
